TPU v7x, 256 devices: a whole 4x4x8 slice. The times are simulated.
256 devices in a mesh: row: 16 (over y_lo, x, core), col: 16 (over y_hi, z).
Axes of the slice: x: 4, y: 4 (y_hi: 2, y_lo: 2; y = y_hi * 2 + y_lo), z: 8, core: 2. Of those that a mesh axis runs over, the one named last changes fastest.
Arguments:
- tiles: bfloat16 [16, 16, 128, 128, 128], P('row', 'col'), as said below
- coords: int32 [16, 16, 2, 128], P('row', 'col'), may hold values from 0 to 63, as said below
- counts: int32 [16, 16], P('row', 'col'), may hold values from 1 to 128, as said below
- valid: int32 [131072], P(('row', 'col')), may hold values 0 or 1
- start: float32 [8, 131072], P(None, ('row', 'col'))
- rotations: float32 [2, 8, 24], replicated, as said below
Outputs:
- eigenmaps: float32 [8, 131072], P(None, ('row', 'col'))
- ritz: float32 [8, 8], replicated
Inputs may be any that keep to these rules, and one draw needn't show every extreme that they name: coords[r, c, 0, s] is a block row from 0 to 63 and coords[r, c, 1, s] a block column from 0 to 63; the live slots of one owner name distinct blocks, each on or above the block diagonal (g_row <= g_col). The live slots of an owner are the first counts[r, c] of its list; one owner in grid row 0 has all 128 live. `tiles`: nonnegative; a tile on the block diagonal is symmetric. The Rayleigh-Ritz coefficients of the current vectors, rotations[t, :, 0 to 7], form a matrix whose diagonal dominates its rows.
All inputs are finite; a program needn't handle non-finite values. No bound on the sum of `valid` on one device may be relied on, other than what follows from the above.
Results may differ from a plain program's by a relative error of at most 0.0013.
Values may be sent and summed in bfloat16 or wider, within the bound.
No kernel may reach another device: no remote copies, remote signals or barrier semaphores. Data moves between devices by JAX's collectives and lax.ppermute only.
A program may use at most 64 MiB of HBM per device.

v0:
```python
import jax
import jax.numpy as jnp
from jax import lax
from jax.sharding import PartitionSpec as P


def matmul_high(left, right):
    return jnp.dot(left, right, precision=lax.Precision.HIGHEST)


def lower_inverse(lower_factor):
    order_size = lower_factor.shape[0]
    identity = jnp.eye(order_size, dtype=lower_factor.dtype)
    inverse_rows = []
    for row_at in range(order_size):
        partial_row = identity[row_at]
        for prior_at in range(row_at):
            partial_row = partial_row - lower_factor[row_at, prior_at] * inverse_rows[prior_at]
        inverse_rows.append(partial_row / lower_factor[row_at, row_at])
    return jnp.stack(inverse_rows)


def settle(new_vecs, new_images, new_steps, step_images, gram_x, gram_ax, node_total):
    lower_factor = jnp.linalg.cholesky(gram_x / node_total)
    inverse = lower_inverse(lower_factor)
    theta = matmul_high(matmul_high(inverse, gram_ax / node_total), inverse.T)
    return (
        matmul_high(inverse, new_vecs),
        matmul_high(inverse, new_images),
        matmul_high(inverse, new_steps),
        matmul_high(inverse, step_images),
        theta,
    )


def gram_sums(new_vecs, new_images):
    return lax.psum(
        (matmul_high(new_vecs, new_vecs.T), matmul_high(new_images, new_vecs.T)), ("row", "col")
    )


def local_terms(
    part_tiles, part_rows, part_cols, weight_direct, weight_mirror, col_blocks, row_blocks
):
    row_span = row_blocks.shape[1]
    col_span = col_blocks.shape[1]
    col_values = jnp.take(col_blocks, part_cols, axis=1)
    row_values = jnp.take(row_blocks, part_rows, axis=1)
    direct = (
        jnp.einsum("sut,cst->csu", part_tiles, col_values, preferred_element_type=jnp.float32)
        * weight_direct[None, :, None]
    )
    mirror = (
        jnp.einsum("sut,csu->cst", part_tiles, row_values, preferred_element_type=jnp.float32)
        * weight_mirror[None, :, None]
    )
    pick_rows = (part_rows[:, None] == jnp.arange(row_span, dtype=jnp.int32)[None, :]).astype(
        jnp.float32
    )
    pick_cols = (part_cols[:, None] == jnp.arange(col_span, dtype=jnp.int32)[None, :]).astype(
        jnp.float32
    )
    rows_sum = jnp.einsum("sp,csu->cpu", pick_rows, direct, precision=lax.Precision.HIGHEST)
    cols_sum = jnp.einsum("sq,cst->cqt", pick_cols, mirror, precision=lax.Precision.HIGHEST)
    return (rows_sum, cols_sum)


def body(tiles, coords, counts, valid, start, rotations):
    row_count = lax.axis_size("row")
    col_count = lax.axis_size("col")
    row_index = lax.axis_index("row")
    col_index = lax.axis_index("col")
    slot_count = tiles.shape[2]
    tile_side = tiles.shape[3]
    stretch_nodes = valid.shape[0]
    per_stretch = stretch_nodes // tile_side
    row_span = col_count * per_stretch
    col_span = row_count * per_stretch
    node_total = jnp.float32(stretch_nodes * row_count * col_count)
    vec_count = start.shape[0]
    flat_tiles = tiles.reshape(slot_count, tile_side, tile_side)
    block_rows = coords[0, 0, 0]
    block_cols = coords[0, 0, 1]
    live_count = counts[0, 0]
    global_rows = row_index * row_span + block_rows
    global_cols = (
        block_cols // per_stretch * col_count + col_index
    ) * per_stretch + block_cols % per_stretch
    live = (jnp.arange(slot_count, dtype=jnp.int32) < live_count).astype(jnp.float32)
    mirror_weight = live * (global_rows != global_cols).astype(jnp.float32)

    def graph_product(vectors):
        width = vectors.shape[0]
        short = vectors.astype(jnp.bfloat16)
        col_side = lax.all_gather(short, "row", axis=1, tiled=True)
        row_side = lax.all_gather(short, "col", axis=1, tiled=True)
        col_blocks = col_side.reshape(width, col_span, tile_side)
        row_blocks = row_side.reshape(width, row_span, tile_side)
        rows_total, cols_total = local_terms(
            flat_tiles, block_rows, block_cols, live, mirror_weight, col_blocks, row_blocks
        )
        direct_part = lax.psum_scatter(
            rows_total.reshape(width, row_span * tile_side), "col", scatter_dimension=1, tiled=True
        )
        mirror_part = lax.psum_scatter(
            cols_total.reshape(width, col_span * tile_side), "row", scatter_dimension=1, tiled=True
        )
        return direct_part + mirror_part

    node_mask = valid.astype(jnp.float32)
    first_vecs = start * node_mask[None, :]
    raw = graph_product(jnp.concatenate([node_mask[None, :], first_vecs], 0))
    degree = raw[0]
    first_images = node_mask[None, :] * (degree[None, :] * first_vecs - raw[1:])
    zero_steps = jnp.zeros_like(first_vecs)
    gram_x, gram_ax = gram_sums(first_vecs, first_images)
    vecs, images, steps, step_images, theta = settle(
        first_vecs, first_images, zero_steps, zero_steps, gram_x, gram_ax, node_total
    )
    for turn in range(rotations.shape[0]):
        resid = images - matmul_high(theta, vecs)
        resid_images = node_mask[None, :] * (degree[None, :] * resid - graph_product(resid))
        stacked = jnp.concatenate([vecs, resid, steps], 0)
        stacked_images = jnp.concatenate([images, resid_images, step_images], 0)
        rotation = rotations[turn]
        new_vecs = matmul_high(rotation, stacked)
        new_images = matmul_high(rotation, stacked_images)
        gram_x, gram_ax = gram_sums(new_vecs, new_images)
        new_steps = matmul_high(rotation[:, vec_count:], stacked[vec_count:])
        new_step_images = matmul_high(rotation[:, vec_count:], stacked_images[vec_count:])
        vecs, images, steps, step_images, theta = settle(
            new_vecs, new_images, new_steps, new_step_images, gram_x, gram_ax, node_total
        )
    return (vecs, theta)


def solution(mesh):
    in_specs = (
        P("row", "col", None, None, None),
        P("row", "col", None, None),
        P("row", "col"),
        P(("row", "col")),
        P(None, ("row", "col")),
        P(),
    )
    out_specs = (P(None, ("row", "col")), P())
    return jax.shard_map(body, mesh=mesh, in_specs=in_specs, out_specs=out_specs, check_vma=False)
```

profile of v0, /device:TPU:1, one launch (start us, length us, event | category | flops | bytes accessed | tf_op | source)
XLA Modules:
  0.0 1272.5 jit_solution(13226586753436208169)
XLA Ops:
  7.2 0.8 compare_and_fusion
  8.0 0.8 slice_bitcast_fusion.2
  8.8 0.7 convert_convert_fusion
  9.5 0.7 multiply_convert_fusion
  10.2 39.4 %all_gather.19 = bf16[9,8192]{1,0:T(8,128)(2,1)S(1)} all-gather(bf16[9,512]{1,0:T(8,128)(2,1)S(1)} %pad_maximum_fusion.8), channel_id=1, replica_groups=mesh['row'=16,'col'=16] {'col'}, dimensions={1}, use_global_device_ids=true | all-gather | bytes 156672 | tf_op jit(solution)/shard_map/all_gather | solution.py:96
  50.5 0.7 gather_fusion.1
  51.2 3.4 fusion.8
  55.3 1.1 copy.34
  56.4 26.8 %all_gather.18 = bf16[9,8192]{1,0:T(8,128)(2,1)S(1)} all-gather(bf16[9,512]{1,0:T(8,128)(2,1)S(1)} %pad_maximum_fusion.8), channel_id=1, replica_groups=mesh['row'=16,'col'=16] {'row'}, dimensions={1}, use_global_device_ids=true | all-gather | bytes 156672 | tf_op jit(solution)/shard_map/all_gather | solution.py:95
  83.4 0.7 gather_fusion
  84.2 4.5 fusion.10
  88.7 0.5 convolution_bitcast_fusion.1
  89.3 1.1 copy.32
  90.7 26.8 %reduce-scatter.9.cloned.1.call-done = f32[9,512]{1,0:T(8,128)} async-done(((f32[9,8192]{1,0:T(8,128)}), f32[9,512]{1,0:T(8,128)}) %reduce-scatter.9.cloned.1.call-update) | async-done | bytes 18448 | tf_op jit(solution)/shard_map/reduce_scatter | solution.py:105
  117.5 198.7 %reduce-scatter.7.cloned.1.call-done = f32[9,512]{1,0:T(8,128)} async-done(((f32[9,8192]{1,0:T(8,128)}), f32[9,512]{1,0:T(8,128)}) %reduce-scatter.7.cloned.1.call-update) | async-done | bytes 18448 | tf_op jit(solution)/shard_map/reduce_scatter | solution.py:102
  316.2 0.8 add.100
  317.1 79.7 %all-reduce.2 = (f32[8,8]{0,1:T(8,128)S(1)}, f32[8,8]{0,1:T(8,128)S(1)}) all-reduce(f32[8,8]{0,1:T(8,128)S(1)} %fusion.95, f32[8,8]{0,1:T(8,128)S(1)} %fusion.87), channel_id=1, replica_groups=mesh['row'=16,'col'=16] {'row','col'}, use_global_device_ids=true, to_apply=%region_0.1 | all-reduce | flops 128 | bytes 1024 | tf_op jit(solution)/shard_map/psum | solution.py:37
  396.9 0.7 cholesky.59
  397.6 0.6 compare_reduce_fusion.2
  398.3 0.6 fusion.110
  398.9 0.7 fusion.147
  399.6 0.7 fusion.148
  400.4 22.6 %subtract_divide_fusion.14 = (f32[1,8]{1,0:T(1,128)S(1)}, f32[1,8]{1,0:T(1,128)S(1)}, f32[1,8]{1,0:T(1,128)S(1)}, f32[1,8]{1,0:T(1,128)S(1)}, f32[1,8]{1,0:T(1,1...) fusion(f32[]{:T(128)} %bitcast.36, f32[]{:T(128)} %bitcast.35, f32[]{:T(128)} %bitcast.34, ...), kind=kLoop, calls=%fused_computation.199 | loop fusion | flops 512 | bytes 656 | tf_op jit(solution)/shard_map/div | solution.py:19
  423.7 31.8 %all_gather.21 = bf16[8,8192]{1,0:T(8,128)(2,1)S(1)} all-gather(bf16[8,512]{1,0:T(8,128)(2,1)S(1)} %get-tuple-element.153), channel_id=1, replica_groups=mesh['row'=16,'col'=16] {'col'}, dimensions={1}, use_global_device_ids=true | all-gather | bytes 139264 | tf_op jit(solution)/shard_map/all_gather | solution.py:96
  455.4 24.9 %all_gather.20 = bf16[8,8192]{1,0:T(8,128)(2,1)S(1)} all-gather(bf16[8,512]{1,0:T(8,128)(2,1)S(1)} %get-tuple-element.153), channel_id=1, replica_groups=mesh['row'=16,'col'=16] {'row'}, dimensions={1}, use_global_device_ids=true | all-gather | bytes 139264 | tf_op jit(solution)/shard_map/all_gather | solution.py:95
  480.4 0.7 gather_fusion.3
  481.1 3.4 fusion.4
  485.0 0.8 copy.69
  485.9 0.7 gather_fusion.2
  486.6 4.5 fusion.6
  491.5 0.9 copy.70
  492.9 0.6 fusion.68
  493.5 45.7 %reduce-scatter.13.cloned.1.call-done = f32[8,512]{1,0:T(8,128)} async-done(((f32[8,8192]{1,0:T(8,128)}), f32[8,512]{1,0:T(8,128)}) %reduce-scatter.13.cloned.1.call-update) | async-done | bytes 16400 | tf_op jit(solution)/shard_map/reduce_scatter | solution.py:105
  539.2 197.1 %reduce-scatter.11.cloned.1.call-done = f32[8,512]{1,0:T(8,128)} async-done(((f32[8,8192]{1,0:T(8,128)}), f32[8,512]{1,0:T(8,128)}) %reduce-scatter.11.cloned.1.call-update) | async-done | bytes 16400 | tf_op jit(solution)/shard_map/reduce_scatter | solution.py:102
  736.3 0.7 subtract_multiply_fusion.1
  737.3 79.8 %all-reduce.1 = (f32[8,8]{0,1:T(8,128)S(1)}, f32[8,8]{0,1:T(8,128)S(1)}) all-reduce(f32[8,8]{0,1:T(8,128)S(1)} %fusion.152, f32[8,8]{0,1:T(8,128)S(1)} %fusion.155), channel_id=1, replica_groups=mesh['row'=16,'col'=16] {'row','col'}, use_global_device_ids=true, to_apply=%region_6.9 | all-reduce | flops 128 | bytes 1024 | tf_op jit(solution)/shard_map/psum | solution.py:37
  817.2 0.7 cholesky.70
  817.9 0.6 compare_reduce_fusion.1
  818.6 0.6 fusion.111
  819.2 0.7 fusion.145
  820.0 0.7 fusion.146
  820.7 22.6 %subtract_divide_fusion.7 = (f32[1,8]{1,0:T(1,128)S(1)}, f32[1,8]{1,0:T(1,128)S(1)}, f32[1,8]{1,0:T(1,128)S(1)}, f32[1,8]{1,0:T(1,128)S(1)}, f32[1,8]{1,0:T(1,12...) fusion(f32[]{:T(128)} %bitcast.87, f32[]{:T(128)} %bitcast.86, f32[]{:T(128)} %bitcast.85, ...), kind=kLoop, calls=%fused_computation.190 | loop fusion | flops 512 | bytes 656 | tf_op jit(solution)/shard_map/div | solution.py:19
  844.0 31.8 %all_gather.23 = bf16[8,8192]{1,0:T(8,128)(2,1)S(1)} all-gather(bf16[8,512]{1,0:T(8,128)(2,1)S(1)} %get-tuple-element.155), channel_id=1, replica_groups=mesh['row'=16,'col'=16] {'col'}, dimensions={1}, use_global_device_ids=true | all-gather | bytes 139264 | tf_op jit(solution)/shard_map/all_gather | solution.py:96
  875.8 24.9 %all_gather.22 = bf16[8,8192]{1,0:T(8,128)(2,1)S(1)} all-gather(bf16[8,512]{1,0:T(8,128)(2,1)S(1)} %get-tuple-element.155), channel_id=1, replica_groups=mesh['row'=16,'col'=16] {'row'}, dimensions={1}, use_global_device_ids=true | all-gather | bytes 139264 | tf_op jit(solution)/shard_map/all_gather | solution.py:95
  900.7 0.7 gather_fusion.5
  901.4 3.4 fusion
  905.3 0.8 copy.67
  906.3 0.7 gather_fusion.4
  906.9 4.5 fusion.2
  911.9 0.9 copy.68
  913.4 0.6 fusion.69
  914.3 45.1 %reduce-scatter.17.cloned.1.call-done = f32[8,512]{1,0:T(8,128)} async-done(((f32[8,8192]{1,0:T(8,128)}), f32[8,512]{1,0:T(8,128)}) %reduce-scatter.17.cloned.1.call-update) | async-done | bytes 16400 | tf_op jit(solution)/shard_map/reduce_scatter | solution.py:105
  959.4 197.2 %reduce-scatter.15.cloned.1.call-done = f32[8,512]{1,0:T(8,128)} async-done(((f32[8,8192]{1,0:T(8,128)}), f32[8,512]{1,0:T(8,128)}) %reduce-scatter.15.cloned.1.call-update) | async-done | bytes 16400 | tf_op jit(solution)/shard_map/reduce_scatter | solution.py:102
  1156.6 0.7 subtract_multiply_fusion
  1157.3 0.6 fusion.62
  1158.2 79.7 %all-reduce = (f32[8,8]{0,1:T(8,128)S(1)}, f32[8,8]{0,1:T(8,128)S(1)}) all-reduce(f32[8,8]{0,1:T(8,128)S(1)} %fusion.158, f32[8,8]{0,1:T(8,128)S(1)} %fusion.161), channel_id=1, replica_groups=mesh['row'=16,'col'=16] {'row','col'}, use_global_device_ids=true, to_apply=%region_10.14 | all-reduce | flops 128 | bytes 1024 | tf_op jit(solution)/shard_map/psum | solution.py:37
  1237.9 0.7 cholesky.81
  1238.7 0.6 compare_reduce_fusion
  1239.3 0.6 select_select_fusion
  1240.0 0.7 fusion.143
  1240.7 0.7 fusion.144
  1241.4 22.6 %subtract_divide_fusion = (f32[1,8]{1,0:T(1,128)S(1)}, f32[1,8]{1,0:T(1,128)S(1)}, f32[1,8]{1,0:T(1,128)S(1)}, f32[1,8]{1,0:T(1,128)S(1)}, f32[1,8]{1,0:T(1,128)...) fusion(f32[]{:T(128)} %bitcast.133, f32[]{:T(128)} %bitcast.132, f32[]{:T(128)} %bitcast.131, ...), kind=kLoop, calls=%fused_computation.183 | loop fusion | flops 512 | bytes 656 | tf_op jit(solution)/shard_map/div | solution.py:19
  1264.0 0.7 fusion.159
  1264.9 0.7 fusion.162
  (77 shorter events, 7.3 us)
Async XLA Ops:
  7.2 47.5 %copy-start.2 = (s32[1,1,2,128]{3,2,1,0:T(2,128)S(1)}, s32[1,1,2,128]{3,2,1,0:T(2,128)}, u32[]{:S(2)}) copy-start(s32[1,1,2,128]{3,2,1,0:T(2,128)} %param.12) | copy-start | bytes 3076
  7.2 110.3 %reduce-scatter.9.cloned.1.call-start = ((), (), s32[]{:S(2)}) async-start(), calls=%async_computation.7 | async-start | bytes 557056 | tf_op jit(solution)/shard_map/reduce_scatter | solution.py:105
  56.4 259.8 %reduce-scatter.7.cloned.1.call-start = ((), (), s32[]{:S(2)}) async-start(), calls=%async_computation.6 | async-start | bytes 557056 | tf_op jit(solution)/shard_map/reduce_scatter | solution.py:102
  84.2 6.3 copy-start.1
  84.2 6.4 copy-start
  90.4 448.7 %reduce-scatter.13.cloned.1.call-start = ((), (), s32[]{:S(2)}) async-start(), calls=%async_computation.9 | async-start | bytes 278528 | tf_op jit(solution)/shard_map/reduce_scatter | solution.py:105
  485.8 250.4 %reduce-scatter.11.cloned.1.call-start = ((), (), s32[]{:S(2)}) async-start(), calls=%async_computation.8 | async-start | bytes 278528 | tf_op jit(solution)/shard_map/reduce_scatter | solution.py:102
  492.5 466.9 %reduce-scatter.17.cloned.1.call-start = ((), (), s32[]{:S(2)}) async-start(), calls=%async_computation.11 | async-start | bytes 278528 | tf_op jit(solution)/shard_map/reduce_scatter | solution.py:105
  906.2 250.4 %reduce-scatter.15.cloned.1.call-start = ((), (), s32[]{:S(2)}) async-start(), calls=%async_computation.10 | async-start | bytes 278528 | tf_op jit(solution)/shard_map/reduce_scatter | solution.py:102
Sparse Core Ops, SparseCore 0:
  56.5 60.9 reduce-scatter.8
  121.8 194.3 reduce-scatter.6
  485.9 53.1 reduce-scatter.12
  543.3 192.9 reduce-scatter.10
  906.3 53.0 reduce-scatter.16
  963.5 193.0 reduce-scatter.14
where the time goes:
time: 1270 us
  waiting for transfers between devices  711 us (56%)
  blocking collectives  419 us (33%)
  other arithmetic  78.4 us (6%)
  matrix products  33.7 us (3%)
  local copies, waits for them, and re-layouts  15.6 us (1%)
  between operations  15.1 us (1%)
    reduce_scatter x3, waiting for transfers between devices, graph_product(): lax.psum_scatter(rows_total.reshape(width, row_span * tile_side), 'col',...  593 us
    psum x3, blocking collectives, gram_sums(): lax.psum((matmul_high(new_vecs, new_vecs.T), matmul_high(new_images, new_...  239 us
    reduce_scatter x3, waiting for transfers between devices, graph_product(): lax.psum_scatter(cols_total.reshape(width, col_span * tile_side), 'row',...  118 us
    all_gather x3, blocking collectives, graph_product(): row_side = lax.all_gather(short, 'col', axis=1, tiled=True)  103 us
    all_gather x3, blocking collectives, graph_product(): col_side = lax.all_gather(short, 'row', axis=1, tiled=True)  76.7 us
    div x3, other arithmetic, lower_inverse(): inverse_rows.append(partial_row / lower_factor[row_at, row_at])  67.8 us
  transfers between devices with their start and end apart: 6, of which 6 were waited for; matrix products, arithmetic and copies ran while one was open for 2% of the time, Pallas kernels for 0%

commit v1 on v0

--- a/solution.py
+++ b/solution.py
@@ -93,7 +93,9 @@
         width = vectors.shape[0]
         short = vectors.astype(jnp.bfloat16)
         col_side = lax.all_gather(short, "row", axis=1, tiled=True)
-        row_side = lax.all_gather(short, "col", axis=1, tiled=True)
+        row_side = jnp.concatenate(
+            lax.all_to_all(jnp.stack([short] * lax.axis_size("col")), "col", 0, 0), axis=1
+        )
         col_blocks = col_side.reshape(width, col_span, tile_side)
         row_blocks = row_side.reshape(width, row_span, tile_side)
         rows_total, cols_total = local_terms(

time: 1270 us -> 1210 us (0.953)
  blocking collectives: 419 us -> 294 us
  waiting for transfers between devices: 711 us -> 749 us
  starting transfers between devices: 0.25 us -> 23.9 us
    all_gather x3 -> x0, blocking collectives: 103 us -> none  [graph_product(): row_side = lax.all_gather(short, 'col', axis=1, tiled=True)]
    reduce_scatter x3, waiting for transfers between devices: 118 us -> 196 us  [graph_product(): lax.psum_scatter(cols_total.reshape(width, col_span * tile_side), 'row',...]
    reduce_scatter x3, waiting for transfers between devices: 593 us -> 549 us  [graph_product(): lax.psum_scatter(rows_total.reshape(width, row_span * tile_side), 'col',...]
    all_to_all x0 -> x3, starting transfers between devices: none -> 23.7 us  [graph_product(): lax.all_to_all(jnp.stack([short] * lax.axis_size('col')), 'col', 0, 0)]
    all_gather x3, blocking collectives: 76.7 us -> 57.2 us  [graph_product(): col_side = lax.all_gather(short, 'row', axis=1, tiled=True)]
  transfers between devices with their start and end apart: 6 -> 9, of which waited for: 6 -> 8; matrix products, arithmetic and copies ran while one was open for 2% -> 3% of each run, Pallas kernels for 0% -> 0%
where the time goes in v1:
time: 1210 us
  waiting for transfers between devices  749 us (62%)
  blocking collectives  294 us (24%)
  other arithmetic  78.2 us (6%)
  matrix products  31.6 us (3%)
  starting transfers between devices  23.9 us (2%)
  local copies, waits for them, and re-layouts  17.8 us (1%)
  between operations  15.1 us (1%)
    reduce_scatter x3, waiting for transfers between devices, graph_product(): lax.psum_scatter(rows_total.reshape(width, row_span * tile_side), 'col',...  549 us
    psum x3, blocking collectives, gram_sums(): lax.psum((matmul_high(new_vecs, new_vecs.T), matmul_high(new_images, new_...  237 us
    reduce_scatter x3, waiting for transfers between devices, graph_product(): lax.psum_scatter(cols_total.reshape(width, col_span * tile_side), 'row',...  196 us
    div x3, other arithmetic, lower_inverse(): inverse_rows.append(partial_row / lower_factor[row_at, row_at])  67.6 us
    all_gather x3, blocking collectives, graph_product(): col_side = lax.all_gather(short, 'row', axis=1, tiled=True)  57.2 us
  transfers between devices with their start and end apart: 9, of which 8 were waited for; matrix products, arithmetic and copies ran while one was open for 3% of the time, Pallas kernels for 0%

profile of v1, /device:TPU:1, one launch (start us, length us, event | category | flops | bytes accessed | tf_op | source)
XLA Modules:
  0.0 1209.9 jit_solution(12387252787781038003)
XLA Ops:
  7.2 0.7 convert_convert_fusion
  7.9 0.7 multiply_convert_fusion
  8.6 0.7 stack.13
  9.3 11.7 all-to-all-start
  21.1 0.8 compare_and_fusion
  21.9 0.8 slice_bitcast_fusion.2
  22.6 20.3 %all_gather.9 = bf16[9,8192]{1,0:T(8,128)(2,1)S(1)} all-gather(bf16[9,512]{1,0:T(8,128)(2,1)S(1)} %pad_maximum_fusion.8), channel_id=1, replica_groups=mesh['row'=16,'col'=16] {'row'}, dimensions={1}, use_global_device_ids=true | all-gather | bytes 156672 | tf_op jit(solution)/shard_map/all_gather | solution.py:95
  43.8 0.7 gather_fusion
  44.5 4.5 fusion.15
  49.6 1.1 copy.53
  51.2 0.7 gather_fusion.1
  51.9 3.5 fusion.21
  55.9 1.1 copy.54
  57.2 185.2 %reduce-scatter.7.cloned.1.call-done = f32[9,512]{1,0:T(8,128)} async-done(((f32[9,8192]{1,0:T(8,128)}), f32[9,512]{1,0:T(8,128)}) %reduce-scatter.7.cloned.1.call-update) | async-done | bytes 18448 | tf_op jit(solution)/shard_map/reduce_scatter | solution.py:104
  242.5 65.7 %reduce-scatter.9.cloned.1.call-done = f32[9,512]{1,0:T(8,128)} async-done(((f32[9,8192]{1,0:T(8,128)}), f32[9,512]{1,0:T(8,128)}) %reduce-scatter.9.cloned.1.call-update) | async-done | bytes 18448 | tf_op jit(solution)/shard_map/reduce_scatter | solution.py:107
  308.1 0.8 add.100
  309.1 78.9 %all-reduce.2 = (f32[8,8]{0,1:T(8,128)S(1)}, f32[8,8]{0,1:T(8,128)S(1)}) all-reduce(f32[8,8]{0,1:T(8,128)S(1)} %fusion.125, f32[8,8]{0,1:T(8,128)S(1)} %fusion.117), channel_id=1, replica_groups=mesh['row'=16,'col'=16] {'row','col'}, use_global_device_ids=true, to_apply=%region_0.1 | all-reduce | flops 128 | bytes 1024 | tf_op jit(solution)/shard_map/psum | solution.py:37
  388.0 0.7 cholesky.59
  388.8 0.6 compare_reduce_fusion.2
  389.4 0.6 fusion.140
  390.1 0.7 fusion.177
  390.8 0.7 fusion.178
  391.5 22.5 %subtract_divide_fusion.14 = (f32[1,8]{1,0:T(1,128)S(1)}, f32[1,8]{1,0:T(1,128)S(1)}, f32[1,8]{1,0:T(1,128)S(1)}, f32[1,8]{1,0:T(1,128)S(1)}, f32[1,8]{1,0:T(1,1...) fusion(f32[]{:T(128)} %bitcast.36, f32[]{:T(128)} %bitcast.35, f32[]{:T(128)} %bitcast.34, ...), kind=kLoop, calls=%fused_computation.199 | loop fusion | flops 512 | bytes 656 | tf_op jit(solution)/shard_map/div | solution.py:19
  414.8 18.4 %all_gather.10 = bf16[8,8192]{1,0:T(8,128)(2,1)S(1)} all-gather(bf16[8,512]{1,0:T(8,128)(2,1)S(1)} %get-tuple-element.153), channel_id=1, replica_groups=mesh['row'=16,'col'=16] {'row'}, dimensions={1}, use_global_device_ids=true | all-gather | bytes 139264 | tf_op jit(solution)/shard_map/all_gather | solution.py:95
  433.2 0.7 stack.15
  433.9 6.0 all-to-all-start.1
  439.9 0.7 gather_fusion.2
  440.6 4.5 fusion.27
  445.5 0.8 copy.78
  446.6 2.2 all-to-all-done.1
  448.8 0.7 gather_fusion.3
  449.5 3.4 fusion.33
  453.3 0.9 copy.77
  454.7 181.7 %reduce-scatter.11.cloned.1.call-done = f32[8,512]{1,0:T(8,128)} async-done(((f32[8,8192]{1,0:T(8,128)}), f32[8,512]{1,0:T(8,128)}) %reduce-scatter.11.cloned.1.call-update) | async-done | bytes 16400 | tf_op jit(solution)/shard_map/reduce_scatter | solution.py:104
  636.4 65.2 %reduce-scatter.13.cloned.1.call-done = f32[8,512]{1,0:T(8,128)} async-done(((f32[8,8192]{1,0:T(8,128)}), f32[8,512]{1,0:T(8,128)}) %reduce-scatter.13.cloned.1.call-update) | async-done | bytes 16400 | tf_op jit(solution)/shard_map/reduce_scatter | solution.py:107
  701.6 0.7 subtract_multiply_fusion.1
  702.7 79.0 %all-reduce.1 = (f32[8,8]{0,1:T(8,128)S(1)}, f32[8,8]{0,1:T(8,128)S(1)}) all-reduce(f32[8,8]{0,1:T(8,128)S(1)} %fusion.182, f32[8,8]{0,1:T(8,128)S(1)} %fusion.185), channel_id=1, replica_groups=mesh['row'=16,'col'=16] {'row','col'}, use_global_device_ids=true, to_apply=%region_6.9 | all-reduce | flops 128 | bytes 1024 | tf_op jit(solution)/shard_map/psum | solution.py:37
  781.7 0.7 cholesky.70
  782.5 0.6 compare_reduce_fusion.1
  783.1 0.6 fusion.141
  783.8 0.7 fusion.175
  784.5 0.7 fusion.176
  785.2 22.5 %subtract_divide_fusion.7 = (f32[1,8]{1,0:T(1,128)S(1)}, f32[1,8]{1,0:T(1,128)S(1)}, f32[1,8]{1,0:T(1,128)S(1)}, f32[1,8]{1,0:T(1,128)S(1)}, f32[1,8]{1,0:T(1,12...) fusion(f32[]{:T(128)} %bitcast.88, f32[]{:T(128)} %bitcast.87, f32[]{:T(128)} %bitcast.86, ...), kind=kLoop, calls=%fused_computation.190 | loop fusion | flops 512 | bytes 656 | tf_op jit(solution)/shard_map/div | solution.py:19
  808.5 18.5 %all_gather.11 = bf16[8,8192]{1,0:T(8,128)(2,1)S(1)} all-gather(bf16[8,512]{1,0:T(8,128)(2,1)S(1)} %get-tuple-element.155), channel_id=1, replica_groups=mesh['row'=16,'col'=16] {'row'}, dimensions={1}, use_global_device_ids=true | all-gather | bytes 139264 | tf_op jit(solution)/shard_map/all_gather | solution.py:95
  826.9 0.7 stack.17
  827.6 5.9 all-to-all-start.2
  833.6 0.7 gather_fusion.4
  834.3 4.5 fusion.39
  839.2 0.8 copy.76
  840.4 2.0 all-to-all-done.2
  842.5 0.7 gather_fusion.5
  843.2 3.4 fusion.45
  847.0 0.9 copy.75
  848.3 181.9 %reduce-scatter.15.cloned.1.call-done = f32[8,512]{1,0:T(8,128)} async-done(((f32[8,8192]{1,0:T(8,128)}), f32[8,512]{1,0:T(8,128)}) %reduce-scatter.15.cloned.1.call-update) | async-done | bytes 16400 | tf_op jit(solution)/shard_map/reduce_scatter | solution.py:104
  1030.2 65.2 %reduce-scatter.17.cloned.1.call-done = f32[8,512]{1,0:T(8,128)} async-done(((f32[8,8192]{1,0:T(8,128)}), f32[8,512]{1,0:T(8,128)}) %reduce-scatter.17.cloned.1.call-update) | async-done | bytes 16400 | tf_op jit(solution)/shard_map/reduce_scatter | solution.py:107
  1095.4 0.7 subtract_multiply_fusion
  1096.4 78.9 %all-reduce = (f32[8,8]{0,1:T(8,128)S(1)}, f32[8,8]{0,1:T(8,128)S(1)}) all-reduce(f32[8,8]{0,1:T(8,128)S(1)} %fusion.188, f32[8,8]{0,1:T(8,128)S(1)} %fusion.191), channel_id=1, replica_groups=mesh['row'=16,'col'=16] {'row','col'}, use_global_device_ids=true, to_apply=%region_10.14 | all-reduce | flops 128 | bytes 1024 | tf_op jit(solution)/shard_map/psum | solution.py:37
  1175.4 0.7 cholesky.81
  1176.8 0.6 select_select_fusion
  1177.4 0.7 fusion.173
  1178.2 0.7 fusion.174
  1178.9 22.5 %subtract_divide_fusion = (f32[1,8]{1,0:T(1,128)S(1)}, f32[1,8]{1,0:T(1,128)S(1)}, f32[1,8]{1,0:T(1,128)S(1)}, f32[1,8]{1,0:T(1,128)S(1)}, f32[1,8]{1,0:T(1,128)...) fusion(f32[]{:T(128)} %bitcast.135, f32[]{:T(128)} %bitcast.134, f32[]{:T(128)} %bitcast.133, ...), kind=kLoop, calls=%fused_computation.183 | loop fusion | flops 512 | bytes 656 | tf_op jit(solution)/shard_map/div | solution.py:19
  1201.4 0.7 fusion.189
  1202.3 0.7 fusion.192
  (83 shorter events, 8.4 us)
Async XLA Ops:
  9.3 41.5 %all-to-all-start = ((bf16[16,9,512]{2,1,0:T(8,128)(2,1)}), bf16[16,9,512]{2,1,0:T(8,128)(2,1)S(1)}, u32[]{:S(2)}, u32[]{:S(2)}) async-start(bf16[16,9,512]{2,1,0:T(8,128)(2,1)} %stack.13), calls=%async_computation.1 | async-start | bytes 524288 | tf_op jit(solution)/shard_map/all_to_all | solution.py:97
  21.1 221.4 %reduce-scatter.7.cloned.1.call-start = ((), (), s32[]{:S(2)}) async-start(), calls=%async_computation.9 | async-start | bytes 557056 | tf_op jit(solution)/shard_map/reduce_scatter | solution.py:104
  44.5 6.3 copy-start.2
  50.7 257.4 %reduce-scatter.9.cloned.1.call-start = ((), (), s32[]{:S(2)}) async-start(), calls=%async_computation.10 | async-start | bytes 557056 | tf_op jit(solution)/shard_map/reduce_scatter | solution.py:107
  51.9 5.2 copy-start.1
  51.9 5.2 copy-start
  433.9 14.9 %all-to-all-start.1 = ((bf16[16,8,512]{2,1,0:T(8,128)(2,1)}), bf16[16,8,512]{2,1,0:T(8,128)(2,1)S(1)}, u32[]{:S(2)}, u32[]{:S(2)}) async-start(bf16[16,8,512]{2,1,0:T(8,128)(2,1)} %stack.15), calls=%async_computation.4 | async-start | bytes 262144 | tf_op jit(solution)/shard_map/all_to_all | solution.py:97
  439.9 196.6 %reduce-scatter.11.cloned.1.call-start = ((), (), s32[]{:S(2)}) async-start(), calls=%async_computation.11 | async-start | bytes 278528 | tf_op jit(solution)/shard_map/reduce_scatter | solution.py:104
  446.4 255.3 %reduce-scatter.13.cloned.1.call-start = ((), (), s32[]{:S(2)}) async-start(), calls=%async_computation.12 | async-start | bytes 278528 | tf_op jit(solution)/shard_map/reduce_scatter | solution.py:107
  827.6 14.9 %all-to-all-start.2 = ((bf16[16,8,512]{2,1,0:T(8,128)(2,1)}), bf16[16,8,512]{2,1,0:T(8,128)(2,1)S(1)}, u32[]{:S(2)}, u32[]{:S(2)}) async-start(bf16[16,8,512]{2,1,0:T(8,128)(2,1)} %stack.17), calls=%async_computation.7 | async-start | bytes 262144 | tf_op jit(solution)/shard_map/all_to_all | solution.py:97
  833.5 196.6 %reduce-scatter.15.cloned.1.call-start = ((), (), s32[]{:S(2)}) async-start(), calls=%async_computation.13 | async-start | bytes 278528 | tf_op jit(solution)/shard_map/reduce_scatter | solution.py:104
  840.0 255.3 %reduce-scatter.17.cloned.1.call-start = ((), (), s32[]{:S(2)}) async-start(), calls=%async_computation.14 | async-start | bytes 278528 | tf_op jit(solution)/shard_map/reduce_scatter | solution.py:107
Sparse Core Ops, SparseCore 0:
  50.9 191.5 reduce-scatter.6
  245.1 62.9 reduce-scatter.8
  446.5 189.8 reduce-scatter.10
  638.9 62.6 reduce-scatter.12
  840.2 189.9 reduce-scatter.14
  1032.7 62.6 reduce-scatter.16
